TPU v7x, 32 devices: a whole 2x2x4 slice. The times are simulated.
32 devices in a mesh: occ: 4 (over z), aux: 4 (over x, core), vir: 2 (over y).
Axes of the slice: x: 2, y: 2, z: 4, core: 2. Of those that a mesh axis runs over, the one named last changes fastest.
Arguments:
- integrals: bfloat16 [4, 2048, 4096], P('occ', 'vir', 'aux'), may hold values from -0.65625 to 0.65625
- occ_energy: float32 [4], replicated, may hold values from -2 to -0.5
- vir_energy: float32 [2048], replicated, may hold values from 0.25 to 3
Outputs:
- lagrangian: bfloat16 [4, 2048, 4096], P('occ', 'vir', 'aux')
All inputs are finite; a program needn't handle non-finite values.
Results may differ from a plain program's by a relative error of at most 0.0039.
Values may be sent and summed in bfloat16 or wider, within the bound.
No kernel may reach another device: no remote copies, remote signals or barrier semaphores. Data moves between devices by JAX's collectives and lax.ppermute only.
A program may use at most 64 MiB of HBM per device.

v0:
```python
import jax
import jax.numpy as jnp
from jax import lax
from jax.sharding import PartitionSpec as P

CHUNKS = 4
AUX_BY_PERMUTE = False
Z_GATED = False


def shifted_2(value, axis, by):
    count = lax.axis_size(axis)
    return lax.ppermute(value, axis, [(i, (i + by) % count) for i in range(count)])


def general_plan(integrals, occ_energy, vir_energy):
    row_count = integrals.shape[0]
    vir_width = integrals.shape[1]
    cycle_size = lax.axis_size("occ")
    position = lax.axis_index("occ")
    own_level = lax.dynamic_slice_in_dim(occ_energy, position * row_count, row_count)
    partner_level = lax.dynamic_slice_in_dim(
        occ_energy, (position - 2) % cycle_size * row_count, row_count
    )
    local_vir = lax.dynamic_slice_in_dim(vir_energy, lax.axis_index("vir") * vir_width, vir_width)
    shifted = shifted_2(integrals, "occ", 2)
    partner = lax.all_gather(shifted, "vir", axis=1, tiled=True)
    virtuals = partner.shape[1]
    pair_level = own_level + partner_level
    share_rows = virtuals // lax.axis_size("aux")
    partial_value = lax.psum_scatter(
        jnp.einsum("nbq,naq->bna", partner, integrals, preferred_element_type=jnp.float32),
        "aux",
        scatter_dimension=0,
        tiled=True,
    )
    first_row = lax.axis_index("aux") * share_rows
    vir_rows = lax.dynamic_slice_in_dim(vir_energy, first_row, share_rows)
    amplitudes = (
        partial_value
        / (pair_level[None, :, None] - vir_rows[:, None, None] - local_vir[None, None, :])
    ).astype(jnp.bfloat16)
    portion = lax.all_gather(amplitudes, "aux", axis=0, tiled=True)
    own_part = jnp.einsum("bna,nbq->naq", portion, partner, preferred_element_type=jnp.float32)
    rows_back = jnp.einsum("bna,naq->nbq", portion, integrals, preferred_element_type=jnp.float32)
    owned = lax.psum_scatter(rows_back, "vir", scatter_dimension=1, tiled=True)
    returned = shifted_2(owned, "occ", -2)
    return (own_part + returned).astype(jnp.bfloat16)


def xor_pairs(count, step):
    return [(j, j ^ step) for j in range(count)]


def aux_reduce_scatter(x):
    count = lax.axis_size("aux")
    k = lax.axis_index("aux")
    first = 0
    step = 1
    while step < count:
        half = x.shape[0] // 2
        bit = k // step % 2
        keep = lax.dynamic_slice_in_dim(x, bit * half, half, 0)
        send = lax.dynamic_slice_in_dim(x, (1 - bit) * half, half, 0)
        x = keep + lax.ppermute(send, "aux", xor_pairs(count, step))
        first = first + bit * half
        step *= 2
    return (x, first)


def aux_all_gather(x):
    count = lax.axis_size("aux")
    k = lax.axis_index("aux")
    step = count // 2
    while step >= 1:
        bit = k // step % 2
        other = lax.ppermute(x, "aux", xor_pairs(count, step))
        x = jnp.where(bit == 0, jnp.concatenate([x, other]), jnp.concatenate([other, x]))
        step //= 2
    return x


def paired_plan(integrals, occ_energy, vir_energy):
    own = integrals[0]
    vir_rows, _ = own.shape
    cycle_size = lax.axis_size("occ")
    position = lax.axis_index("occ")
    pair_level = occ_energy[position] + occ_energy[(position - 2) % cycle_size]
    vir_pos = lax.axis_index("vir")
    vir_count = lax.axis_size("vir")
    aux_count = lax.axis_size("aux")
    share = vir_rows // aux_count
    width = vir_rows // CHUNKS
    if not AUX_BY_PERMUTE:
        first_row = lax.axis_index("aux") * share

    def forward(c, arrived):
        if vir_count == 2:
            mate = shifted_2(arrived, "vir", 1)
            block = jnp.concatenate([arrived, mate])
            cols = [vir_pos, 1 - vir_pos]
        else:
            block = lax.all_gather(arrived, "vir", axis=0, tiled=True)
            cols = list(range(vir_count))
        col_level = jnp.concatenate(
            [lax.dynamic_slice_in_dim(vir_energy, w * vir_rows + c * width, width) for w in cols]
        )
        return (block, col_level)

    def reduce(block):
        partial = jnp.einsum("aq,bq->ab", own, block, preferred_element_type=jnp.float32)
        if AUX_BY_PERMUTE:
            return aux_reduce_scatter(partial)
        return (lax.psum_scatter(partial, "aux", scatter_dimension=0, tiled=True), first_row)

    def amplitudes_of(summed, first, col_level):
        row_level = lax.dynamic_slice_in_dim(vir_energy, vir_pos * vir_rows + first, share)
        amplitudes = (summed / (pair_level - row_level[:, None] - col_level[None, :])).astype(
            jnp.bfloat16
        )
        if AUX_BY_PERMUTE:
            return aux_all_gather(amplitudes)
        return lax.all_gather(amplitudes, "aux", axis=0, tiled=True)

    arrived = [None] * CHUNKS
    blocks = [None] * CHUNKS
    levels = [None] * CHUNKS
    summed = [None] * CHUNKS
    firsts = [None] * CHUNKS
    gathered = [None] * CHUNKS
    total = None
    for c in range(CHUNKS if not Z_GATED else 0):
        arrived[c] = shifted_2(own[c * width : (c + 1) * width], "occ", 2)
    for t in range(CHUNKS + 4):
        piece = own[t * width : (t + 1) * width] if Z_GATED and t < CHUNKS else None
        if t > 0:
            gate = {"arrived": arrived[t - 1] if t - 1 < CHUNKS else None}
            if piece is not None:
                gate["piece"] = piece
            if 0 <= t - 2 < CHUNKS:
                gate["block"] = blocks[t - 2]
            if 0 <= t - 3 < CHUNKS:
                gate["summed"] = summed[t - 3]
            if 0 <= t - 4 < CHUNKS:
                gate["gathered"] = gathered[t - 4]
            if total is not None:
                gate["total"] = total
            gate = lax.optimization_barrier(gate)
            if piece is not None:
                piece = gate["piece"]
            if t - 1 < CHUNKS:
                arrived[t - 1] = gate["arrived"]
            if 0 <= t - 2 < CHUNKS:
                blocks[t - 2] = gate["block"]
            if 0 <= t - 3 < CHUNKS:
                summed[t - 3] = gate["summed"]
            if 0 <= t - 4 < CHUNKS:
                gathered[t - 4] = gate["gathered"]
            if total is not None:
                total = gate["total"]
        if piece is not None:
            arrived[t] = shifted_2(piece, "occ", 2)
        c = t - 1
        if 0 <= c < CHUNKS:
            blocks[c], levels[c] = forward(c, arrived[c])
        c = t - 2
        if 0 <= c < CHUNKS:
            summed[c], firsts[c] = reduce(blocks[c])
        c = t - 3
        if 0 <= c < CHUNKS:
            gathered[c] = amplitudes_of(summed[c], firsts[c], levels[c])
        c = t - 4
        if 0 <= c < CHUNKS:
            term = jnp.dot(gathered[c], blocks[c], preferred_element_type=jnp.float32)
            total = term if total is None else total + term
    gamma_own = total
    gamma_back = total
    return (gamma_own + gamma_back).astype(jnp.bfloat16)[None]


def on_device(integrals, occ_energy, vir_energy):
    cycle_size = lax.axis_size("occ")
    if integrals.shape[0] == 1 and 4 % cycle_size == 0 and (integrals.shape[1] % (CHUNKS * 8) == 0):
        return paired_plan(integrals, occ_energy, vir_energy)
    return general_plan(integrals, occ_energy, vir_energy)


def solution(mesh):
    placed = (P("occ", "vir", "aux"), P(), P())
    return jax.shard_map(
        on_device, mesh=mesh, in_specs=placed, out_specs=P("occ", "vir", "aux"), check_vma=False
    )
```

profile of v0, /device:TPU:0, one launch (start us, length us, event | category | flops | bytes accessed | tf_op | source)
XLA Modules:
  0.0 284.6 jit_solution(10130402411361232367)
XLA Ops:
  6.5 2.7 slice_bitcast_fusion
  9.2 4.0 %collective-permute-start.3 = (bf16[256,1024]{1,0:T(8,128)(2,1)S(1)}, bf16[256,1024]{1,0:T(8,128)(2,1)S(1)}, u32[]{:S(2)}, u32[]{:S(2)}) collective-permute-start(bf16[256,1024]{1,0:T(8,128)(2,1)S(1)} %get-tuple-element.41), channel_id=1, source_target_pairs={{0,16},{8,24},{16,0},{24,8},{1,17},{9,25},{17,1},{25,9},{2,18},{10... | collective-permute-start | bytes 1572872 | tf_op jit(solution)/shard_map/ppermute | solution.py:13
  13.3 23.2 %collective-permute-done.3 = bf16[256,1024]{1,0:T(8,128)(2,1)S(1)} collective-permute-done((bf16[256,1024]{1,0:T(8,128)(2,1)S(1)}, bf16[256,1024]{1,0:T(8,128)(2,1)S(1)}, u32[]{:S(2)}, u32[]{:S(2)}) %collective-permute-start.3) | collective-permute-done | bytes 524320 | tf_op jit(solution)/shard_map/ppermute | solution.py:13
  38.0 11.5 %collective-permute-done.4 = bf16[256,1024]{1,0:T(8,128)(2,1)S(1)} collective-permute-done((bf16[256,1024]{1,0:T(8,128)(2,1)S(1)}, bf16[256,1024]{1,0:T(8,128)(2,1)S(1)}, u32[]{:S(2)}, u32[]{:S(2)}) %collective-permute-start.4) | collective-permute-done | bytes 524320 | tf_op jit(solution)/shard_map/ppermute | solution.py:13
  49.6 13.1 %collective-permute-done.2 = bf16[256,1024]{1,0:T(8,128)(2,1)S(1)} collective-permute-done((bf16[256,1024]{1,0:T(8,128)(2,1)S(1)}, bf16[256,1024]{1,0:T(8,128)(2,1)S(1)}, u32[]{:S(2)}, u32[]{:S(2)}) %collective-permute-start.2) | collective-permute-done | bytes 524320 | tf_op jit(solution)/shard_map/ppermute | solution.py:13
  62.7 2.6 fusion.8
  68.2 9.3 %collective-permute-done.5 = bf16[256,1024]{1,0:T(8,128)(2,1)} collective-permute-done((bf16[256,1024]{1,0:T(8,128)(2,1)S(1)}, bf16[256,1024]{1,0:T(8,128)(2,1)}, u32[]{:S(2)}, u32[]{:S(2)}) %collective-permute-start.5) | collective-permute-done | bytes 524320 | tf_op jit(solution)/shard_map/ppermute | solution.py:13
  78.5 11.8 %collective-permute-done.1 = bf16[256,1024]{1,0:T(8,128)(2,1)S(1)} collective-permute-done((bf16[256,1024]{1,0:T(8,128)(2,1)}, bf16[256,1024]{1,0:T(8,128)(2,1)S(1)}, u32[]{:S(2)}, u32[]{:S(2)}) %collective-permute-start.1) | collective-permute-done | bytes 524320 | tf_op jit(solution)/shard_map/ppermute | solution.py:13
  90.4 4.3 %reduce-scatter.5.cloned.1.call-done = f32[256,512]{0,1:T(8,128)} async-done(((f32[1024,512]{0,1:T(8,128)}), f32[256,512]{0,1:T(8,128)}) %reduce-scatter.5.cloned.1.call-update) | async-done | bytes 524304 | tf_op jit(solution)/shard_map/reduce_scatter | solution.py:114
  96.7 4.2 %fusion.11 = f32[1024,512]{0,1:T(8,128)} fusion(bf16[512,1024]{1,0:T(8,128)(2,1)S(1)} %pad_maximum_fusion.1, bf16[1,1024,1024]{2,1,0:T(8,128)(2,1)} %param.3), kind=kOutput, calls=%fused_computation.11 | convolution fusion | flops 1073741824 | bytes 5242880 | tf_op jit(solution)/shard_map/aq,bq->ab/dot_general | solution.py:111
  104.9 9.8 %collective-permute-done.6 = bf16[256,1024]{1,0:T(8,128)(2,1)S(1)} collective-permute-done((bf16[256,1024]{1,0:T(8,128)(2,1)S(1)}, bf16[256,1024]{1,0:T(8,128)(2,1)S(1)}, u32[]{:S(2)}, u32[]{:S(2)}) %collective-permute-start.6) | collective-permute-done | bytes 524320 | tf_op jit(solution)/shard_map/ppermute | solution.py:13
  115.8 12.5 %collective-permute-done = bf16[256,1024]{1,0:T(8,128)(2,1)} collective-permute-done((bf16[256,1024]{1,0:T(8,128)(2,1)}, bf16[256,1024]{1,0:T(8,128)(2,1)}, u32[]{:S(2)}, u32[]{:S(2)}) %collective-permute-start) | collective-permute-done | bytes 524320 | tf_op jit(solution)/shard_map/ppermute | solution.py:13
  128.4 19.4 %reduce-scatter.7.cloned.1.call-done = f32[256,512]{0,1:T(8,128)} async-done(((f32[1024,512]{0,1:T(8,128)}), f32[256,512]{0,1:T(8,128)}) %reduce-scatter.7.cloned.1.call-update) | async-done | bytes 524304 | tf_op jit(solution)/shard_map/reduce_scatter | solution.py:114
  149.8 4.2 %fusion.14 = f32[1024,512]{0,1:T(8,128)} fusion(bf16[512,1024]{1,0:T(8,128)(2,1)S(1)} %pad_maximum_fusion.2, bf16[1,1024,1024]{2,1,0:T(8,128)(2,1)} %param.3), kind=kOutput, calls=%fused_computation.12 | convolution fusion | flops 1073741824 | bytes 5242880 | tf_op jit(solution)/shard_map/aq,bq->ab/dot_general | solution.py:111
  155.6 4.5 %fusion.23 = f32[1024,1024]{1,0:T(8,128)} fusion(bf16[1024,512]{0,1:T(8,128)(2,1)} %all-gather.5.cloned.1.call-done, bf16[512,1024]{1,0:T(8,128)(2,1)S(1)} %pad_maximum_fusion), kind=kOutput, calls=%fused_computation.34 | convolution fusion | flops 1073741824 | bytes 6291456 | tf_op jit(solution)/shard_map/dot_general | solution.py:174
  160.1 7.9 %collective-permute-done.7 = bf16[256,1024]{1,0:T(8,128)(2,1)S(1)} collective-permute-done((bf16[256,1024]{1,0:T(8,128)(2,1)}, bf16[256,1024]{1,0:T(8,128)(2,1)S(1)}, u32[]{:S(2)}, u32[]{:S(2)}) %collective-permute-start.7) | collective-permute-done | bytes 524320 | tf_op jit(solution)/shard_map/ppermute | solution.py:13
  169.1 31.4 %reduce-scatter.9.cloned.1.call-done = f32[256,512]{0,1:T(8,128)} async-done(((f32[1024,512]{0,1:T(8,128)}), f32[256,512]{0,1:T(8,128)}) %reduce-scatter.9.cloned.1.call-update) | async-done | bytes 524304 | tf_op jit(solution)/shard_map/reduce_scatter | solution.py:114
  202.6 4.2 %fusion.17 = f32[1024,512]{0,1:T(8,128)} fusion(bf16[512,1024]{1,0:T(8,128)(2,1)S(1)} %pad_maximum_fusion.3, bf16[1,1024,1024]{2,1,0:T(8,128)(2,1)} %param.3), kind=kOutput, calls=%fused_computation.13 | convolution fusion | flops 1073741824 | bytes 5242880 | tf_op jit(solution)/shard_map/aq,bq->ab/dot_general | solution.py:111
  210.3 2.9 %add.120 = f32[1024,1024]{1,0:T(8,128)} add(f32[1024,1024]{1,0:T(8,128)S(1)} %copy-done, f32[1024,1024]{1,0:T(8,128)S(1)} %fusion.24) | non-fusion elementwise | flops 1048576 | bytes 12582912 | tf_op jit(solution)/shard_map/add | solution.py:175
  213.2 6.3 %all-gather.9.cloned.1.call-done = bf16[1024,512]{0,1:T(8,128)(2,1)} async-done(((bf16[256,512]{0,1:T(8,128)(2,1)}), bf16[1024,512]{0,1:T(8,128)(2,1)}) %all-gather.9.cloned.1.call-update) | async-done | bytes 1048592 | tf_op jit(solution)/shard_map/all_gather | solution.py:123
  219.5 34.1 %reduce-scatter.11.cloned.1.call-done = f32[256,512]{0,1:T(8,128)} async-done(((f32[1024,512]{0,1:T(8,128)}), f32[256,512]{0,1:T(8,128)}) %reduce-scatter.11.cloned.1.call-update) | async-done | bytes 524304 | tf_op jit(solution)/shard_map/reduce_scatter | solution.py:114
  255.6 5.5 %convolution_add_fusion = f32[1024,1024]{1,0:T(8,128)} fusion(f32[1024,1024]{1,0:T(8,128)} %add.120, bf16[1024,512]{0,1:T(8,128)(2,1)S(1)} %copy-done.1, bf16[512,1024]{1,0:T(8,128)(2,1)S(1)} %pad_maximum_fusion.2), kind=kOutput, calls=%fused_computation.1 | convolution fusion | flops 1074790400 | bytes 10485760 | tf_op jit(solution)/shard_map/dot_general | solution.py:174
  261.1 11.5 %all-gather.11.cloned.1.call-done = bf16[1024,512]{0,1:T(8,128)(2,1)} async-done(((bf16[256,512]{0,1:T(8,128)(2,1)}), bf16[1024,512]{0,1:T(8,128)(2,1)}) %all-gather.11.cloned.1.call-update) | async-done | bytes 1048592 | tf_op jit(solution)/shard_map/all_gather | solution.py:123
  272.6 5.1 %fusion.20 = bf16[1,1024,1024]{2,1,0:T(8,128)(2,1)} fusion(f32[1024,1024]{1,0:T(8,128)} %convolution_add_fusion, bf16[1024,512]{0,1:T(8,128)(2,1)} %all-gather.11.cloned.1.call-done, bf16[512,1024]{1,0:T(8,128)(2,1)S(1)} %copy-done.5), kind=kOutput, calls=%fused_computation.14 | convolution fusion | flops 1076887552 | bytes 8388608 | tf_op jit(solution)/shard_map/dot_general | solution.py:174
  (58 shorter events, 23.6 us)
Async XLA Ops:
  6.5 88.2 %reduce-scatter.5.cloned.1.call-start = ((), (), s32[]{:S(2)}) async-start(), calls=%async_computation.4 | async-start | bytes 2621440 | tf_op jit(solution)/shard_map/reduce_scatter | solution.py:114
  9.2 53.4 %copy-start.2 = (bf16[1,1024,1024]{2,1,0:T(8,128)(2,1)S(1)}, bf16[1,1024,1024]{2,1,0:T(8,128)(2,1)}, u32[]{:S(2)}) copy-start(bf16[1,1024,1024]{2,1,0:T(8,128)(2,1)} %param.3) | copy-start | bytes 6291460
  9.2 27.2 %collective-permute-start.3 = (bf16[256,1024]{1,0:T(8,128)(2,1)S(1)}, bf16[256,1024]{1,0:T(8,128)(2,1)S(1)}, u32[]{:S(2)}, u32[]{:S(2)}) collective-permute-start(bf16[256,1024]{1,0:T(8,128)(2,1)S(1)} %get-tuple-element.41), channel_id=1, source_target_pairs={{0,16},{8,24},{16,0},{24,8},{1,17},{9,25},{17,1},{25,9},{2,18},{10... | collective-permute-start | bytes 1572872 | tf_op jit(solution)/shard_map/ppermute | solution.py:13
  36.4 13.1 %collective-permute-start.4 = (bf16[256,1024]{1,0:T(8,128)(2,1)S(1)}, bf16[256,1024]{1,0:T(8,128)(2,1)S(1)}, u32[]{:S(2)}, u32[]{:S(2)}) collective-permute-start(bf16[256,1024]{1,0:T(8,128)(2,1)S(1)} %collective-permute-done.3), channel_id=1, source_target_pairs={{0,1},{1,0},{2,3},{3,2},{4,5},{5,4},{6,7},{7,6},{8,9},{9,8},{10,11... | collective-permute-start | bytes 1572872 | tf_op jit(solution)/shard_map/ppermute | solution.py:13
  38.0 24.7 %collective-permute-start.2 = (bf16[256,1024]{1,0:T(8,128)(2,1)S(1)}, bf16[256,1024]{1,0:T(8,128)(2,1)S(1)}, u32[]{:S(2)}, u32[]{:S(2)}) collective-permute-start(bf16[256,1024]{1,0:T(8,128)(2,1)S(1)} %get-tuple-element.42), channel_id=1, source_target_pairs={{0,16},{8,24},{16,0},{24,8},{1,17},{9,25},{17,1},{25,9},{2,18},{10... | collective-permute-start | bytes 1572872 | tf_op jit(solution)/shard_map/ppermute | solution.py:13
  65.3 2.7 copy-start.7
  65.3 63.1 %all-gather.5.cloned.1.call-start = ((), (), s32[]{:S(2)}) async-start(), calls=%async_computation.5 | async-start | bytes 1310720 | tf_op jit(solution)/shard_map/all_gather | solution.py:123
  65.4 12.1 %collective-permute-start.5 = (bf16[256,1024]{1,0:T(8,128)(2,1)S(1)}, bf16[256,1024]{1,0:T(8,128)(2,1)}, u32[]{:S(2)}, u32[]{:S(2)}) collective-permute-start(bf16[256,1024]{1,0:T(8,128)(2,1)S(1)} %collective-permute-done.2), channel_id=1, source_target_pairs={{0,1},{1,0},{2,3},{3,2},{4,5},{5,4},{6,7},{7,6},{8,9},{9,8},{10,11... | collective-permute-start | bytes 1572872 | tf_op jit(solution)/shard_map/ppermute | solution.py:13
  66.2 24.2 %collective-permute-start.1 = (bf16[256,1024]{1,0:T(8,128)(2,1)}, bf16[256,1024]{1,0:T(8,128)(2,1)S(1)}, u32[]{:S(2)}, u32[]{:S(2)}) collective-permute-start(bf16[256,1024]{1,0:T(8,128)(2,1)} %get-tuple-element.43), channel_id=1, source_target_pairs={{0,16},{8,24},{16,0},{24,8},{1,17},{9,25},{17,1},{25,9},{2,18},{10... | collective-permute-start | bytes 1572872 | tf_op jit(solution)/shard_map/ppermute | solution.py:13
  90.4 10.6 %copy-start.6 = (bf16[256,1024]{1,0:T(8,128)(2,1)}, bf16[256,1024]{1,0:T(8,128)(2,1)S(1)}, u32[]{:S(2)}) copy-start(bf16[256,1024]{1,0:T(8,128)(2,1)S(1)} %collective-permute-done.1) | copy-start | bytes 1572868
  96.6 51.2 %reduce-scatter.7.cloned.1.call-start = ((), (), s32[]{:S(2)}) async-start(), calls=%async_computation.6 | async-start | bytes 2621440 | tf_op jit(solution)/shard_map/reduce_scatter | solution.py:114
  100.9 68.2 %all-gather.7.cloned.1.call-start = ((), (), s32[]{:S(2)}) async-start(), calls=%async_computation.7 | async-start | bytes 1310720 | tf_op jit(solution)/shard_map/all_gather | solution.py:123
  101.0 13.8 %collective-permute-start.6 = (bf16[256,1024]{1,0:T(8,128)(2,1)S(1)}, bf16[256,1024]{1,0:T(8,128)(2,1)S(1)}, u32[]{:S(2)}, u32[]{:S(2)}) collective-permute-start(bf16[256,1024]{1,0:T(8,128)(2,1)S(1)} %collective-permute-done.1), channel_id=1, source_target_pairs={{0,1},{1,0},{2,3},{3,2},{4,5},{5,4},{6,7},{7,6},{8,9},{9,8},{10,11... | collective-permute-start | bytes 1572872 | tf_op jit(solution)/shard_map/ppermute | solution.py:13
  102.5 25.8 %collective-permute-start = (bf16[256,1024]{1,0:T(8,128)(2,1)}, bf16[256,1024]{1,0:T(8,128)(2,1)}, u32[]{:S(2)}, u32[]{:S(2)}) collective-permute-start(bf16[256,1024]{1,0:T(8,128)(2,1)} %get-tuple-element.44), channel_id=1, source_target_pairs={{0,16},{8,24},{16,0},{24,8},{1,17},{9,25},{17,1},{25,9},{2,18},{10... | collective-permute-start | bytes 1572872 | tf_op jit(solution)/shard_map/ppermute | solution.py:13
  149.7 50.9 %reduce-scatter.9.cloned.1.call-start = ((), (), s32[]{:S(2)}) async-start(), calls=%async_computation.8 | async-start | bytes 2621440 | tf_op jit(solution)/shard_map/reduce_scatter | solution.py:114
  154.0 65.5 %all-gather.9.cloned.1.call-start = ((), (), s32[]{:S(2)}) async-start(), calls=%async_computation.9 | async-start | bytes 1310720 | tf_op jit(solution)/shard_map/all_gather | solution.py:123
  154.0 13.9 %collective-permute-start.7 = (bf16[256,1024]{1,0:T(8,128)(2,1)}, bf16[256,1024]{1,0:T(8,128)(2,1)S(1)}, u32[]{:S(2)}, u32[]{:S(2)}) collective-permute-start(bf16[256,1024]{1,0:T(8,128)(2,1)} %collective-permute-done), channel_id=1, source_target_pairs={{0,1},{1,0},{2,3},{3,2},{4,5},{5,4},{6,7},{7,6},{8,9},{9,8},{10,11... | collective-permute-start | bytes 1572872 | tf_op jit(solution)/shard_map/ppermute | solution.py:13
  169.1 33.5 %copy-start.4 = (bf16[512,1024]{1,0:T(8,128)(2,1)}, bf16[512,1024]{1,0:T(8,128)(2,1)S(1)}, u32[]{:S(2)}) copy-start(bf16[512,1024]{1,0:T(8,128)(2,1)S(1)} %pad_maximum_fusion.3) | copy-start | bytes 3145732
  202.5 51.2 %reduce-scatter.11.cloned.1.call-start = ((), (), s32[]{:S(2)}) async-start(), calls=%async_computation.10 | async-start | bytes 2621440 | tf_op jit(solution)/shard_map/reduce_scatter | solution.py:114
  206.8 1.2 copy-start.3
  206.8 65.8 %all-gather.11.cloned.1.call-start = ((), (), s32[]{:S(2)}) async-start(), calls=%async_computation.11 | async-start | bytes 1310720 | tf_op jit(solution)/shard_map/all_gather | solution.py:123
  208.0 2.3 copy-start
  219.5 36.1 %copy-start.1 = (bf16[1024,512]{0,1:T(8,128)(2,1)S(1)}, bf16[1024,512]{0,1:T(8,128)(2,1)}, u32[]{:S(2)}) copy-start(bf16[1024,512]{0,1:T(8,128)(2,1)} %all-gather.9.cloned.1.call-done) | copy-start | bytes 3145732
  255.6 17.0 %copy-start.5 = (bf16[512,1024]{1,0:T(8,128)(2,1)S(1)}, bf16[512,1024]{1,0:T(8,128)(2,1)}, u32[]{:S(2)}) copy-start(bf16[512,1024]{1,0:T(8,128)(2,1)} %copy-done.4) | copy-start | bytes 3145732
  (1 other events, 0.9 us)
Sparse Core Ops, SparseCore 0:
  65.4 29.2 reduce-scatter.4
  96.8 16.8 all-gather.4
  116.3 31.4 reduce-scatter.6
  149.8 16.8 all-gather.6
  169.1 31.4 reduce-scatter.8
  202.6 16.8 all-gather.8
  222.2 31.4 reduce-scatter.10
  255.7 16.8 all-gather.10
where the time goes:
time: 285 us
  waiting for transfers between devices  206 us (72%)
  matrix products  31.7 us (11%)
  between operations  14.8 us (5%)
  other arithmetic  14 us (5%)
  starting transfers between devices  12.4 us (4%)
  local copies, waits for them, and re-layouts  5.35 us (2%)
    ppermute x8, waiting for transfers between devices, shifted_2(): lax.ppermute(value, axis, [(i, (i + by) % count) for i in range(count)])  99 us
    reduce_scatter x4, waiting for transfers between devices, reduce(): lax.psum_scatter(partial, 'aux', scatter_dimension=0, tiled=True)  89.4 us
    all_gather x4, waiting for transfers between devices, amplitudes_of(): return lax.all_gather(amplitudes, 'aux', axis=0, tiled=True)  17.8 us
    dot_general x4, matrix products, paired_plan(): term = jnp.dot(gathered[c], blocks[c], preferred_element_type=jnp.float32)  16.5 us
    dot_general x4, matrix products, reduce(): jnp.einsum('aq,bq->ab', own, block, preferred_element_type=jnp.float32)  15.2 us
    ppermute x8, starting transfers between devices, shifted_2(): lax.ppermute(value, axis, [(i, (i + by) % count) for i in range(count)])  11.9 us
    convert_element_type x4, other arithmetic, amplitudes_of(): (summed / (pair_level - row_level[:, None] - col_level[None, :])).astype(...  7.58 us
  transfers between devices with their start and end apart: 16, of which 14 were waited for; matrix products, arithmetic and copies ran while one was open for 11% of the time, Pallas kernels for 0%

commit v1 on v0

--- a/solution.py
+++ b/solution.py
@@ -6,6 +6,22 @@
 CHUNKS = 4
 AUX_BY_PERMUTE = False
 Z_GATED = False
+
+
+def ring_gather(x, axis, dim):
+    ways, here, step = (lax.axis_size(axis), lax.axis_index(axis), x.shape[dim])
+    dims = [n * ways if d == dim else n for d, n in enumerate(x.shape)]
+    full = lax.dynamic_update_slice_in_dim(jnp.zeros(dims, x.dtype), x, here * step, axis=dim)
+    going_up = going_down = x
+    for far in range(1, ways // 2 + 1):
+        going_up = lax.ppermute(going_up, axis, [(d, (d + 1) % ways) for d in range(ways)])
+        full = lax.dynamic_update_slice_in_dim(full, going_up, (here - far) % ways * step, axis=dim)
+        if 2 * far < ways:
+            going_down = lax.ppermute(going_down, axis, [(d, (d - 1) % ways) for d in range(ways)])
+            full = lax.dynamic_update_slice_in_dim(
+                full, going_down, (here + far) % ways * step, axis=dim
+            )
+    return full
 
 
 def shifted_2(value, axis, by):
@@ -120,7 +136,7 @@
         )
         if AUX_BY_PERMUTE:
             return aux_all_gather(amplitudes)
-        return lax.all_gather(amplitudes, "aux", axis=0, tiled=True)
+        return ring_gather(amplitudes, "aux", 0)
 
     arrived = [None] * CHUNKS
     blocks = [None] * CHUNKS

time: 285 us -> 227 us (0.80)
  waiting for transfers between devices: 206 us -> 151 us
  matrix products: 31.7 us -> 22 us
  starting transfers between devices: 12.4 us -> 19.2 us
    reduce_scatter x4, waiting for transfers between devices: 89.4 us -> 34.2 us  [reduce(): lax.psum_scatter(partial, 'aux', scatter_dimension=0, tiled=True)]
    ppermute x0 -> x12, waiting for transfers between devices: none -> 25.4 us  [the longest x8 25.3 us: ring_gather(): lax.ppermute(going_up, axis, [(d, (d + 1) % ways) for d in range(ways)])]
    all_gather x4 -> x0, waiting for transfers between devices: 17.8 us -> none  [amplitudes_of(): return lax.all_gather(amplitudes, 'aux', axis=0, tiled=True)]
    dot_general x4, matrix products: 16.5 us -> 8.4 us  [paired_plan(): term = jnp.dot(gathered[c], blocks[c], preferred_element_type=jnp.float32)]
    convert_element_type x4 -> x0, other arithmetic: 7.58 us -> none  [amplitudes_of(): (summed / (pair_level - row_level[:, None] - col_level[None, :])).astype(...]
    ppermute x8, waiting for transfers between devices: 99 us -> 91.7 us  [shifted_2(): lax.ppermute(value, axis, [(i, (i + by) % count) for i in range(count)])]
    ppermute x0 -> x12, starting transfers between devices: none -> 7.26 us  [the longest x4 6.97 us: ring_gather(): lax.ppermute(going_down, axis, [(d, (d - 1) % ways) for d in range(ways)])]
    dynamic_update_slice x0 -> x4, other arithmetic: none -> 3.71 us  [ring_gather(): lax.dynamic_update_slice_in_dim(jnp.zeros(dims, x.dtype), x, here * step,...]
  transfers between devices with their start and end apart: 16 -> 24, of which waited for: 14 -> 18; matrix products, arithmetic and copies ran while one was open for 11% -> 8% of each run, Pallas kernels for 0% -> 0%
where the time goes in v1:
time: 227 us; the launch traced here: 226 us
  waiting for transfers between devices  151 us (67%)
  matrix products  22 us (10%)
  starting transfers between devices  19.2 us (8%)
  between operations  14.9 us (7%)
  other arithmetic  14.3 us (6%)
  local copies, waits for them, and re-layouts  4.72 us (2%)
    ppermute x8, waiting for transfers between devices, shifted_2(): lax.ppermute(value, axis, [(i, (i + by) % count) for i in range(count)])  91.7 us
    reduce_scatter x4, waiting for transfers between devices, reduce(): lax.psum_scatter(partial, 'aux', scatter_dimension=0, tiled=True)  34.2 us
    ppermute x8, waiting for transfers between devices, ring_gather(): lax.ppermute(going_up, axis, [(d, (d + 1) % ways) for d in range(ways)])  25.3 us
    dot_general x4, matrix products, reduce(): jnp.einsum('aq,bq->ab', own, block, preferred_element_type=jnp.float32)  13.6 us
    ppermute x8, starting transfers between devices, shifted_2(): lax.ppermute(value, axis, [(i, (i + by) % count) for i in range(count)])  11.8 us
    dot_general x4, matrix products, paired_plan(): term = jnp.dot(gathered[c], blocks[c], preferred_element_type=jnp.float32)  8.4 us
    ppermute x4, starting transfers between devices, ring_gather(): lax.ppermute(going_down, axis, [(d, (d - 1) % ways) for d in range(ways)])  6.97 us
  transfers between devices with their start and end apart: 24, of which 18 were waited for; matrix products, arithmetic and copies ran while one was open for 8% of the time, Pallas kernels for 0%

profile of v1, /device:TPU:0, one launch (start us, length us, event | category | flops | bytes accessed | tf_op | source)
XLA Modules:
  0.0 226.4 jit_solution(8714905639595808330)
XLA Ops:
  6.5 2.7 %slice_bitcast_fusion = (bf16[256,1024]{1,0:T(8,128)(2,1)S(1)}, bf16[256,1024]{1,0:T(8,128)(2,1)S(1)}, bf16[256,1024]{1,0:T(8,128)(2,1)}, bf16[256,1024]{1,0:T(8,128)(2,1)}) fusion(bf16[1,1024,1024]{2,1,0:T(8,128)(2,1)} %param.3), kind=kLoop, calls=%fused_computation.22 | loop fusion | bytes 4194304 | tf_op jit(solution)/shard_map/slice | solution.py:149
  9.2 4.0 %collective-permute-start.3 = (bf16[256,1024]{1,0:T(8,128)(2,1)S(1)}, bf16[256,1024]{1,0:T(8,128)(2,1)S(1)}, u32[]{:S(2)}, u32[]{:S(2)}) collective-permute-start(bf16[256,1024]{1,0:T(8,128)(2,1)S(1)} %get-tuple-element.49), channel_id=1, source_target_pairs={{0,16},{8,24},{16,0},{24,8},{1,17},{9,25},{17,1},{25,9},{2,18},{10... | collective-permute-start | bytes 1572872 | tf_op jit(solution)/shard_map/ppermute | solution.py:29
  13.3 23.2 %collective-permute-done.3 = bf16[256,1024]{1,0:T(8,128)(2,1)S(1)} collective-permute-done((bf16[256,1024]{1,0:T(8,128)(2,1)S(1)}, bf16[256,1024]{1,0:T(8,128)(2,1)S(1)}, u32[]{:S(2)}, u32[]{:S(2)}) %collective-permute-start.3) | collective-permute-done | bytes 524320 | tf_op jit(solution)/shard_map/ppermute | solution.py:29
  38.0 11.5 %collective-permute-done.4 = bf16[256,1024]{1,0:T(8,128)(2,1)S(1)} collective-permute-done((bf16[256,1024]{1,0:T(8,128)(2,1)S(1)}, bf16[256,1024]{1,0:T(8,128)(2,1)S(1)}, u32[]{:S(2)}, u32[]{:S(2)}) %collective-permute-start.4) | collective-permute-done | bytes 524320 | tf_op jit(solution)/shard_map/ppermute | solution.py:29
  49.6 13.2 %collective-permute-done.2 = bf16[256,1024]{1,0:T(8,128)(2,1)} collective-permute-done((bf16[256,1024]{1,0:T(8,128)(2,1)S(1)}, bf16[256,1024]{1,0:T(8,128)(2,1)}, u32[]{:S(2)}, u32[]{:S(2)}) %collective-permute-start.2) | collective-permute-done | bytes 524320 | tf_op jit(solution)/shard_map/ppermute | solution.py:29
  62.8 2.6 %fusion.9 = f32[1024,512]{0,1:T(8,128)} fusion(bf16[512,1024]{1,0:T(8,128)(2,1)S(1)} %pad_maximum_fusion, bf16[1,1024,1024]{2,1,0:T(8,128)(2,1)S(1)} %copy-done.7), kind=kOutput, calls=%fused_computation.10 | convolution fusion | flops 1073741824 | bytes 5242880 | tf_op jit(solution)/shard_map/aq,bq->ab/dot_general | solution.py:127
  66.3 11.3 %collective-permute-done.5 = bf16[256,1024]{1,0:T(8,128)(2,1)S(1)} collective-permute-done((bf16[256,1024]{1,0:T(8,128)(2,1)}, bf16[256,1024]{1,0:T(8,128)(2,1)S(1)}, u32[]{:S(2)}, u32[]{:S(2)}) %collective-permute-start.5) | collective-permute-done | bytes 524320 | tf_op jit(solution)/shard_map/ppermute | solution.py:29
  78.7 11.8 %collective-permute-done.1 = bf16[256,1024]{1,0:T(8,128)(2,1)} collective-permute-done((bf16[256,1024]{1,0:T(8,128)(2,1)}, bf16[256,1024]{1,0:T(8,128)(2,1)}, u32[]{:S(2)}, u32[]{:S(2)}) %collective-permute-start.1) | collective-permute-done | bytes 524320 | tf_op jit(solution)/shard_map/ppermute | solution.py:29
  90.6 4.3 %reduce-scatter.5.cloned.1.call-done = f32[256,512]{0,1:T(8,128)} async-done(((f32[1024,512]{0,1:T(8,128)}), f32[256,512]{0,1:T(8,128)}) %reduce-scatter.5.cloned.1.call-update) | async-done | bytes 524304 | tf_op jit(solution)/shard_map/reduce_scatter | solution.py:130
  94.9 2.6 %fusion.12 = f32[1024,512]{0,1:T(8,128)} fusion(bf16[512,1024]{1,0:T(8,128)(2,1)S(1)} %pad_maximum_fusion.1, bf16[1,1024,1024]{2,1,0:T(8,128)(2,1)S(1)} %copy-done.7), kind=kOutput, calls=%fused_computation.11 | convolution fusion | flops 1073741824 | bytes 5242880 | tf_op jit(solution)/shard_map/aq,bq->ab/dot_general | solution.py:127
  106.3 3.6 %collective-permute-done.7 = bf16[256,512]{0,1:T(8,128)(2,1)S(1)} collective-permute-done((bf16[256,512]{0,1:T(8,128)(2,1)S(1)}, bf16[256,512]{0,1:T(8,128)(2,1)S(1)}, u32[]{:S(2)}, u32[]{:S(2)}) %collective-permute-start.7) | collective-permute-done | bytes 262176 | tf_op jit(solution)/shard_map/ppermute | solution.py:17
  110.0 4.4 %collective-permute-done.6 = bf16[256,1024]{1,0:T(8,128)(2,1)} collective-permute-done((bf16[256,1024]{1,0:T(8,128)(2,1)}, bf16[256,1024]{1,0:T(8,128)(2,1)}, u32[]{:S(2)}, u32[]{:S(2)}) %collective-permute-start.6) | collective-permute-done | bytes 524320 | tf_op jit(solution)/shard_map/ppermute | solution.py:29
  115.8 13.4 %collective-permute-done = bf16[256,1024]{1,0:T(8,128)(2,1)} collective-permute-done((bf16[256,1024]{1,0:T(8,128)(2,1)}, bf16[256,1024]{1,0:T(8,128)(2,1)}, u32[]{:S(2)}, u32[]{:S(2)}) %collective-permute-start) | collective-permute-done | bytes 524320 | tf_op jit(solution)/shard_map/ppermute | solution.py:29
  129.1 4.2 %fusion.15 = f32[1024,512]{0,1:T(8,128)} fusion(bf16[512,1024]{1,0:T(8,128)(2,1)S(1)} %pad_maximum_fusion.2, bf16[1,1024,1024]{2,1,0:T(8,128)(2,1)} %param.3), kind=kOutput, calls=%fused_computation.12 | convolution fusion | flops 1073741824 | bytes 5242880 | tf_op jit(solution)/shard_map/aq,bq->ab/dot_general | solution.py:127
  137.9 3.6 %collective-permute-done.11 = bf16[256,512]{0,1:T(8,128)(2,1)S(1)} collective-permute-done((bf16[256,512]{0,1:T(8,128)(2,1)S(1)}, bf16[256,512]{0,1:T(8,128)(2,1)S(1)}, u32[]{:S(2)}, u32[]{:S(2)}) %collective-permute-start.11) | collective-permute-done | bytes 262176 | tf_op jit(solution)/shard_map/ppermute | solution.py:17
  141.6 4.5 %fusion.23 = f32[1024,1024]{1,0:T(8,128)} fusion(bf16[1024,512]{0,1:T(8,128)(2,1)S(1)} %constant_dynamic-update-slice_fusion.12, bf16[512,1024]{1,0:T(8,128)(2,1)} %copy-done.2), kind=kOutput, calls=%fused_computation.49 | convolution fusion | flops 1073741824 | bytes 6291456 | tf_op jit(solution)/shard_map/dot_general | solution.py:190
  147.4 3.0 %collective-permute-done.10 = bf16[256,1024]{1,0:T(8,128)(2,1)S(1)} collective-permute-done((bf16[256,1024]{1,0:T(8,128)(2,1)}, bf16[256,1024]{1,0:T(8,128)(2,1)S(1)}, u32[]{:S(2)}, u32[]{:S(2)}) %collective-permute-start.10) | collective-permute-done | bytes 524320 | tf_op jit(solution)/shard_map/ppermute | solution.py:29
  151.6 13.5 %reduce-scatter.9.cloned.1.call-done = f32[256,512]{0,1:T(8,128)} async-done(((f32[1024,512]{0,1:T(8,128)}), f32[256,512]{0,1:T(8,128)}) %reduce-scatter.9.cloned.1.call-update) | async-done | bytes 524304 | tf_op jit(solution)/shard_map/reduce_scatter | solution.py:130
  165.0 4.2 %fusion.18 = f32[1024,512]{0,1:T(8,128)} fusion(bf16[512,1024]{1,0:T(8,128)(2,1)S(1)} %pad_maximum_fusion.3, bf16[1,1024,1024]{2,1,0:T(8,128)(2,1)} %param.3), kind=kOutput, calls=%fused_computation.13 | convolution fusion | flops 1073741824 | bytes 5242880 | tf_op jit(solution)/shard_map/aq,bq->ab/dot_general | solution.py:127
  172.4 6.2 %collective-permute-done.14 = bf16[256,512]{0,1:T(8,128)(2,1)S(1)} collective-permute-done((bf16[256,512]{0,1:T(8,128)(2,1)S(1)}, bf16[256,512]{0,1:T(8,128)(2,1)S(1)}, u32[]{:S(2)}, u32[]{:S(2)}) %collective-permute-start.14) | collective-permute-done | bytes 262176 | tf_op jit(solution)/shard_map/ppermute | solution.py:17
  179.9 2.9 %add.178 = f32[1024,1024]{1,0:T(8,128)} add(f32[1024,1024]{1,0:T(8,128)S(1)} %copy-done, f32[1024,1024]{1,0:T(8,128)S(1)} %fusion.24) | non-fusion elementwise | flops 1048576 | bytes 12582912 | tf_op jit(solution)/shard_map/add | solution.py:191
  184.4 16.5 %reduce-scatter.11.cloned.1.call-done = f32[256,512]{0,1:T(8,128)} async-done(((f32[1024,512]{0,1:T(8,128)}), f32[256,512]{0,1:T(8,128)}) %reduce-scatter.11.cloned.1.call-update) | async-done | bytes 524304 | tf_op jit(solution)/shard_map/reduce_scatter | solution.py:130
  204.0 6.3 %collective-permute-done.17 = bf16[256,512]{0,1:T(8,128)(2,1)S(1)} collective-permute-done((bf16[256,512]{0,1:T(8,128)(2,1)S(1)}, bf16[256,512]{0,1:T(8,128)(2,1)S(1)}, u32[]{:S(2)}, u32[]{:S(2)}) %collective-permute-start.17) | collective-permute-done | bytes 262176 | tf_op jit(solution)/shard_map/ppermute | solution.py:17
  213.1 3.0 %collective-permute-done.19 = bf16[256,512]{0,1:T(8,128)(2,1)S(1)} collective-permute-done((bf16[256,512]{0,1:T(8,128)(2,1)S(1)}, bf16[256,512]{0,1:T(8,128)(2,1)S(1)}, u32[]{:S(2)}, u32[]{:S(2)}) %collective-permute-start.19) | collective-permute-done | bytes 262176 | tf_op jit(solution)/shard_map/ppermute | solution.py:17
  (92 shorter events, 35.2 us)
Async XLA Ops:
  6.5 88.3 %reduce-scatter.5.cloned.1.call-start = ((), (), s32[]{:S(2)}) async-start(), calls=%async_computation.4 | async-start | bytes 2621440 | tf_op jit(solution)/shard_map/reduce_scatter | solution.py:130
  9.2 27.2 %collective-permute-start.3 = (bf16[256,1024]{1,0:T(8,128)(2,1)S(1)}, bf16[256,1024]{1,0:T(8,128)(2,1)S(1)}, u32[]{:S(2)}, u32[]{:S(2)}) collective-permute-start(bf16[256,1024]{1,0:T(8,128)(2,1)S(1)} %get-tuple-element.49), channel_id=1, source_target_pairs={{0,16},{8,24},{16,0},{24,8},{1,17},{9,25},{17,1},{25,9},{2,18},{10... | collective-permute-start | bytes 1572872 | tf_op jit(solution)/shard_map/ppermute | solution.py:29
  36.4 13.1 %collective-permute-start.4 = (bf16[256,1024]{1,0:T(8,128)(2,1)S(1)}, bf16[256,1024]{1,0:T(8,128)(2,1)S(1)}, u32[]{:S(2)}, u32[]{:S(2)}) collective-permute-start(bf16[256,1024]{1,0:T(8,128)(2,1)S(1)} %collective-permute-done.3), channel_id=1, source_target_pairs={{0,1},{1,0},{2,3},{3,2},{4,5},{5,4},{6,7},{7,6},{8,9},{9,8},{10,11... | collective-permute-start | bytes 1572872 | tf_op jit(solution)/shard_map/ppermute | solution.py:29
  38.0 24.8 %collective-permute-start.2 = (bf16[256,1024]{1,0:T(8,128)(2,1)S(1)}, bf16[256,1024]{1,0:T(8,128)(2,1)}, u32[]{:S(2)}, u32[]{:S(2)}) collective-permute-start(bf16[256,1024]{1,0:T(8,128)(2,1)S(1)} %get-tuple-element.50), channel_id=1, source_target_pairs={{0,16},{8,24},{16,0},{24,8},{1,17},{9,25},{17,1},{25,9},{2,18},{10... | collective-permute-start | bytes 1572872 | tf_op jit(solution)/shard_map/ppermute | solution.py:29
  65.4 63.7 %reduce-scatter.7.cloned.1.call-start = ((), (), s32[]{:S(2)}) async-start(), calls=%async_computation.5 | async-start | bytes 2621440 | tf_op jit(solution)/shard_map/reduce_scatter | solution.py:130
  65.5 12.2 %collective-permute-start.5 = (bf16[256,1024]{1,0:T(8,128)(2,1)}, bf16[256,1024]{1,0:T(8,128)(2,1)S(1)}, u32[]{:S(2)}, u32[]{:S(2)}) collective-permute-start(bf16[256,1024]{1,0:T(8,128)(2,1)} %collective-permute-done.2), channel_id=1, source_target_pairs={{0,1},{1,0},{2,3},{3,2},{4,5},{5,4},{6,7},{7,6},{8,9},{9,8},{10,11... | collective-permute-start | bytes 1572872 | tf_op jit(solution)/shard_map/ppermute | solution.py:29
  66.3 24.3 %collective-permute-start.1 = (bf16[256,1024]{1,0:T(8,128)(2,1)}, bf16[256,1024]{1,0:T(8,128)(2,1)}, u32[]{:S(2)}, u32[]{:S(2)}) collective-permute-start(bf16[256,1024]{1,0:T(8,128)(2,1)} %get-tuple-element.51), channel_id=1, source_target_pairs={{0,16},{8,24},{16,0},{24,8},{1,17},{9,25},{17,1},{25,9},{2,18},{10... | collective-permute-start | bytes 1572872 | tf_op jit(solution)/shard_map/ppermute | solution.py:29
  97.5 67.5 %reduce-scatter.9.cloned.1.call-start = ((), (), s32[]{:S(2)}) async-start(), calls=%async_computation.6 | async-start | bytes 2621440 | tf_op jit(solution)/shard_map/reduce_scatter | solution.py:130
  100.3 14.0 %collective-permute-start.6 = (bf16[256,1024]{1,0:T(8,128)(2,1)}, bf16[256,1024]{1,0:T(8,128)(2,1)}, u32[]{:S(2)}, u32[]{:S(2)}) collective-permute-start(bf16[256,1024]{1,0:T(8,128)(2,1)} %collective-permute-done.1), channel_id=1, source_target_pairs={{0,1},{1,0},{2,3},{3,2},{4,5},{5,4},{6,7},{7,6},{8,9},{9,8},{10,11... | collective-permute-start | bytes 1572872 | tf_op jit(solution)/shard_map/ppermute | solution.py:29
  102.1 7.8 %collective-permute-start.7 = (bf16[256,512]{0,1:T(8,128)(2,1)S(1)}, bf16[256,512]{0,1:T(8,128)(2,1)S(1)}, u32[]{:S(2)}, u32[]{:S(2)}) collective-permute-start(bf16[256,512]{0,1:T(8,128)(2,1)S(1)} %get-tuple-element.48), channel_id=1, source_target_pairs={{0,2},{2,4},{4,6},{6,0},{1,3},{3,5},{5,7},{7,1},{8,10},{10,12},{12... | collective-permute-start | bytes 786440 | tf_op jit(solution)/shard_map/ppermute | solution.py:17
  102.1 7.8 %collective-permute-start.8 = (bf16[256,512]{0,1:T(8,128)(2,1)S(1)}, bf16[256,512]{0,1:T(8,128)(2,1)S(1)}, u32[]{:S(2)}, u32[]{:S(2)}) collective-permute-start(bf16[256,512]{0,1:T(8,128)(2,1)S(1)} %get-tuple-element.48), channel_id=1, source_target_pairs={{0,6},{2,0},{4,2},{6,4},{1,7},{3,1},{5,3},{7,5},{8,14},{10,8},{12,... | collective-permute-start | bytes 786440 | tf_op jit(solution)/shard_map/ppermute | solution.py:20
  103.9 25.2 %collective-permute-start = (bf16[256,1024]{1,0:T(8,128)(2,1)}, bf16[256,1024]{1,0:T(8,128)(2,1)}, u32[]{:S(2)}, u32[]{:S(2)}) collective-permute-start(bf16[256,1024]{1,0:T(8,128)(2,1)} %get-tuple-element.52), channel_id=1, source_target_pairs={{0,16},{8,24},{16,0},{24,8},{1,17},{9,25},{17,1},{25,9},{2,18},{10... | collective-permute-start | bytes 1572872 | tf_op jit(solution)/shard_map/ppermute | solution.py:29
  109.9 5.8 %collective-permute-start.9 = (bf16[256,512]{0,1:T(8,128)(2,1)S(1)}, bf16[256,512]{0,1:T(8,128)(2,1)S(1)}, u32[]{:S(2)}, u32[]{:S(2)}) collective-permute-start(bf16[256,512]{0,1:T(8,128)(2,1)S(1)} %collective-permute-done.7), channel_id=1, source_target_pairs={{0,2},{2,4},{4,6},{6,0},{1,3},{3,5},{5,7},{7,1},{8,10},{10,12},{12... | collective-permute-start | bytes 786440 | tf_op jit(solution)/shard_map/ppermute | solution.py:17
  133.3 67.6 %reduce-scatter.11.cloned.1.call-start = ((), (), s32[]{:S(2)}) async-start(), calls=%async_computation.7 | async-start | bytes 2621440 | tf_op jit(solution)/shard_map/reduce_scatter | solution.py:130
  134.7 6.8 %collective-permute-start.11 = (bf16[256,512]{0,1:T(8,128)(2,1)S(1)}, bf16[256,512]{0,1:T(8,128)(2,1)S(1)}, u32[]{:S(2)}, u32[]{:S(2)}) collective-permute-start(bf16[256,512]{0,1:T(8,128)(2,1)S(1)} %get-tuple-element.46), channel_id=1, source_target_pairs={{0,2},{2,4},{4,6},{6,0},{1,3},{3,5},{5,7},{7,1},{8,10},{10,12},{12... | collective-permute-start | bytes 786440 | tf_op jit(solution)/shard_map/ppermute | solution.py:17
  134.8 11.4 %collective-permute-start.12 = (bf16[256,512]{0,1:T(8,128)(2,1)S(1)}, bf16[256,512]{0,1:T(8,128)(2,1)S(1)}, u32[]{:S(2)}, u32[]{:S(2)}) collective-permute-start(bf16[256,512]{0,1:T(8,128)(2,1)S(1)} %get-tuple-element.46), channel_id=1, source_target_pairs={{0,6},{2,0},{4,2},{6,4},{1,7},{3,1},{5,3},{7,5},{8,14},{10,8},{12,... | collective-permute-start | bytes 786440 | tf_op jit(solution)/shard_map/ppermute | solution.py:20
  136.5 13.9 %collective-permute-start.10 = (bf16[256,1024]{1,0:T(8,128)(2,1)}, bf16[256,1024]{1,0:T(8,128)(2,1)S(1)}, u32[]{:S(2)}, u32[]{:S(2)}) collective-permute-start(bf16[256,1024]{1,0:T(8,128)(2,1)} %collective-permute-done), channel_id=1, source_target_pairs={{0,1},{1,0},{2,3},{3,2},{4,5},{5,4},{6,7},{7,6},{8,9},{9,8},{10,11... | collective-permute-start | bytes 1572872 | tf_op jit(solution)/shard_map/ppermute | solution.py:29
  141.6 5.8 %collective-permute-start.13 = (bf16[256,512]{0,1:T(8,128)(2,1)S(1)}, bf16[256,512]{0,1:T(8,128)(2,1)S(1)}, u32[]{:S(2)}, u32[]{:S(2)}) collective-permute-start(bf16[256,512]{0,1:T(8,128)(2,1)S(1)} %collective-permute-done.11), channel_id=1, source_target_pairs={{0,2},{2,4},{4,6},{6,0},{1,3},{3,5},{5,7},{7,1},{8,10},{10,12},{12... | collective-permute-start | bytes 786440 | tf_op jit(solution)/shard_map/ppermute | solution.py:17
  170.6 8.0 %collective-permute-start.14 = (bf16[256,512]{0,1:T(8,128)(2,1)S(1)}, bf16[256,512]{0,1:T(8,128)(2,1)S(1)}, u32[]{:S(2)}, u32[]{:S(2)}) collective-permute-start(bf16[256,512]{0,1:T(8,128)(2,1)S(1)} %get-tuple-element.44), channel_id=1, source_target_pairs={{0,2},{2,4},{4,6},{6,0},{1,3},{3,5},{5,7},{7,1},{8,10},{10,12},{12... | collective-permute-start | bytes 786440 | tf_op jit(solution)/shard_map/ppermute | solution.py:17
  170.7 12.2 %collective-permute-start.15 = (bf16[256,512]{0,1:T(8,128)(2,1)S(1)}, bf16[256,512]{0,1:T(8,128)(2,1)S(1)}, u32[]{:S(2)}, u32[]{:S(2)}) collective-permute-start(bf16[256,512]{0,1:T(8,128)(2,1)S(1)} %get-tuple-element.44), channel_id=1, source_target_pairs={{0,6},{2,0},{4,2},{6,4},{1,7},{3,1},{5,3},{7,5},{8,14},{10,8},{12,... | collective-permute-start | bytes 786440 | tf_op jit(solution)/shard_map/ppermute | solution.py:20
  178.6 5.8 %collective-permute-start.16 = (bf16[256,512]{0,1:T(8,128)(2,1)S(1)}, bf16[256,512]{0,1:T(8,128)(2,1)S(1)}, u32[]{:S(2)}, u32[]{:S(2)}) collective-permute-start(bf16[256,512]{0,1:T(8,128)(2,1)S(1)} %collective-permute-done.14), channel_id=1, source_target_pairs={{0,2},{2,4},{4,6},{6,0},{1,3},{3,5},{5,7},{7,1},{8,10},{10,12},{12... | collective-permute-start | bytes 786440 | tf_op jit(solution)/shard_map/ppermute | solution.py:17
  202.2 8.1 %collective-permute-start.17 = (bf16[256,512]{0,1:T(8,128)(2,1)S(1)}, bf16[256,512]{0,1:T(8,128)(2,1)S(1)}, u32[]{:S(2)}, u32[]{:S(2)}) collective-permute-start(bf16[256,512]{0,1:T(8,128)(2,1)S(1)} %get-tuple-element.42), channel_id=1, source_target_pairs={{0,2},{2,4},{4,6},{6,0},{1,3},{3,5},{5,7},{7,1},{8,10},{10,12},{12... | collective-permute-start | bytes 786440 | tf_op jit(solution)/shard_map/ppermute | solution.py:17
  202.3 10.7 %collective-permute-start.18 = (bf16[256,512]{0,1:T(8,128)(2,1)S(1)}, bf16[256,512]{0,1:T(8,128)(2,1)S(1)}, u32[]{:S(2)}, u32[]{:S(2)}) collective-permute-start(bf16[256,512]{0,1:T(8,128)(2,1)S(1)} %get-tuple-element.42), channel_id=1, source_target_pairs={{0,6},{2,0},{4,2},{6,4},{1,7},{3,1},{5,3},{7,5},{8,14},{10,8},{12,... | collective-permute-start | bytes 786440 | tf_op jit(solution)/shard_map/ppermute | solution.py:20
  210.3 5.8 %collective-permute-start.19 = (bf16[256,512]{0,1:T(8,128)(2,1)S(1)}, bf16[256,512]{0,1:T(8,128)(2,1)S(1)}, u32[]{:S(2)}, u32[]{:S(2)}) collective-permute-start(bf16[256,512]{0,1:T(8,128)(2,1)S(1)} %collective-permute-done.17), channel_id=1, source_target_pairs={{0,2},{2,4},{4,6},{6,0},{1,3},{3,5},{5,7},{7,1},{8,10},{10,12},{12... | collective-permute-start | bytes 786440 | tf_op jit(solution)/shard_map/ppermute | solution.py:17
  (11 other events, 163.9 us)
Sparse Core Ops, SparseCore 0:
  65.5 29.2 reduce-scatter.4
  97.6 31.3 reduce-scatter.6
  133.5 31.5 reduce-scatter.8
  169.4 31.4 reduce-scatter.10
